TPU v7x, 512 devices: a whole 4x8x8 slice. The times are simulated.
512 devices in a mesh: seq: 128 (over x, z_hi, y, core), tp: 4 (over z_lo).
Axes of the slice: x: 4, y: 8, z: 8 (z_hi: 2, z_lo: 4; z = z_hi * 4 + z_lo), core: 2. Of those that a mesh axis runs over, the one named last changes fastest.
Arguments:
- queries: bfloat16 [16384, 4096], P('seq', 'tp'), may hold values from -6 to 6
- suffix_entries: bfloat16 [16384, 4096], P('seq', 'tp'), may hold values from -6 to 6
- prefix_cache: bfloat16 [2048, 4096], P(('seq', 'tp')), may hold values from -6 to 6
- block_prefix: int32 [512], replicated, may hold values from 0 to 1, as said below
- request_lengths: int32 [512], P('seq'), may hold values from 0 to 128, as said below
- request_prefix: int32 [512], P('seq'), may hold values from 0 to 1
Outputs:
- attended: bfloat16 [16384, 4096], P('seq', 'tp')
Inputs may be any that keep to these rules, and one draw needn't show every extreme that they name: `request_lengths`: the lengths of one index of seq's requests sum to at most 128; at some index they sum to exactly 128, and there one request alone takes all 128 slots. `block_prefix`: exactly half of the blocks belong to each prefix.
All inputs are finite; a program needn't handle non-finite values.
Results may differ from a plain program's by a relative error of at most 0.0049.
Values may be sent and summed in bfloat16 or wider, within the bound.
No kernel may reach another device: no remote copies, remote signals or barrier semaphores. Data moves between devices by JAX's collectives and lax.ppermute only.
A program may use at most 64 MiB of HBM per device.

v0:
```python
import math
import jax
import jax.numpy as jnp
import numpy as np
from jax import lax
from jax.sharding import Mesh
from jax.sharding import PartitionSpec as P

HEADS = 16
HEAD = 128
masked_score = -1e30
SEQ_PARTS = (("x", 4), ("zh", 2), ("y", 8), ("core", 2))
STAGES = (("x", "zh", "y"), ("core",))
TP_FIRST = "a2a"


def block_table(stages, per_block_rows, tensor_count):
    names = [n for n, _ in SEQ_PARTS]
    sizes = [s for _, s in SEQ_PARTS]
    coords = np.indices(sizes).reshape(len(sizes), -1).T
    seq_index = np.ravel_multi_index(coords.T, sizes)
    local = {}
    for c, s in zip(map(tuple, coords), seq_index):
        blocks = s * tensor_count + np.arange(tensor_count)
        local[c] = np.repeat(blocks, per_block_rows)
    gathered = set()
    for stage in stages:
        axes = [names.index(n) for n in stage]
        new = {}
        for c in local:
            parts = []
            for sub in np.ndindex(*[sizes[a] for a in axes]):
                other = list(c)
                for a, v in zip(axes, sub):
                    other[a] = v
                parts.append(local[tuple(other)])
            new[c] = np.concatenate(parts)
        local = new
        gathered.update(stage)
    tables = {tuple(v) for v in local.values()}
    assert len(tables) == 1
    return np.asarray(tables.pop(), np.int32)


def token_layout(lengths, prefixes, slots):
    cumulative = jnp.cumsum(lengths)
    slot_ids = jnp.arange(slots, dtype=jnp.int32)
    request_ids = jnp.sum((slot_ids[:, None] >= cumulative[None, :]).astype(jnp.int32), axis=1)
    live_slots = slot_ids < cumulative[-1]
    onehot = request_ids[:, None] == jnp.arange(lengths.shape[0], dtype=jnp.int32)[None, :]
    token_group = jnp.sum(jnp.where(onehot, prefixes[None, :], 0), axis=1)
    return (slot_ids, request_ids, live_slots, token_group)


def per_device(
    queries, suffix_entries, prefix_cache, block_prefix, request_lengths, request_prefix
):
    tensor_count = lax.axis_size("tp")
    local_heads = HEADS // tensor_count
    token_rows = queries.shape[0]
    block_rows = prefix_cache.shape[0]
    column_count = prefix_cache.shape[1] // tensor_count
    slot_ids, request_ids, live_slots, token_group = token_layout(
        request_lengths, request_prefix, token_rows
    )
    if TP_FIRST == "a2a":
        mine = lax.all_to_all(prefix_cache, "tp", split_axis=1, concat_axis=0, tiled=True)
    else:
        whole = lax.all_gather(prefix_cache, "tp", axis=0, tiled=True)
        start = lax.axis_index("tp") * column_count
        mine = lax.dynamic_slice_in_dim(whole, start, column_count, 1)
    for stage in STAGES:
        mine = lax.all_gather(mine, stage, axis=0, tiled=True)
    cached = mine.reshape(-1, local_heads, 2, HEAD)
    table = jnp.asarray(block_table(STAGES, block_rows, tensor_count))
    owners = jnp.take(block_prefix, table)
    query_rows = queries.reshape(token_rows, local_heads, 2, HEAD)
    own_entries = suffix_entries.reshape(token_rows, local_heads, 2, HEAD)
    scale = 1.0 / math.sqrt(HEAD)
    prefix_scores = (
        jnp.einsum(
            "thed,phd->thep", query_rows, cached[:, :, 0], preferred_element_type=jnp.float32
        )
        * scale
    )
    suffix_scores = (
        jnp.einsum(
            "thed,uhd->theu", query_rows, own_entries[:, :, 0], preferred_element_type=jnp.float32
        )
        * scale
    )
    prefix_allowed = ((token_group[:, None] == owners[None, :]) & live_slots[:, None])[
        :, None, None, :
    ]
    suffix_allowed = (
        (request_ids[:, None] == request_ids[None, :])
        & (slot_ids[None, :] <= slot_ids[:, None])
        & live_slots[:, None]
    )[:, None, None, :]
    prefix_scores = jnp.where(prefix_allowed, prefix_scores, masked_score)
    suffix_scores = jnp.where(suffix_allowed, suffix_scores, masked_score)
    row_max = jnp.maximum(jnp.max(prefix_scores, axis=-1), jnp.max(suffix_scores, axis=-1))
    prefix_weight = jnp.where(prefix_allowed, jnp.exp(prefix_scores - row_max[..., None]), 0.0)
    suffix_weight = jnp.where(suffix_allowed, jnp.exp(suffix_scores - row_max[..., None]), 0.0)
    total_weight = jnp.sum(prefix_weight, axis=-1) + jnp.sum(suffix_weight, axis=-1)
    weighted = jnp.einsum(
        "thep,phd->thed",
        prefix_weight.astype(jnp.bfloat16),
        cached[:, :, 1],
        preferred_element_type=jnp.float32,
    )
    weighted = weighted + jnp.einsum(
        "theu,uhd->thed",
        suffix_weight.astype(jnp.bfloat16),
        own_entries[:, :, 1],
        preferred_element_type=jnp.float32,
    )
    live_grid = live_slots[:, None, None]
    safe_total = jnp.where(live_grid, total_weight, 1.0)
    result = jnp.where(live_grid[..., None], weighted / safe_total[..., None], 0.0)
    return result.astype(jnp.bfloat16).reshape(token_rows, local_heads * 2 * HEAD)


def solution(mesh):
    sizes = tuple((s for _, s in SEQ_PARTS)) + (mesh.shape["tp"],)
    names = tuple((n for n, _ in SEQ_PARTS)) + ("tp",)
    fine = Mesh(mesh.devices.reshape(sizes), names)
    seq = names[:-1]
    in_specs = (P(seq, "tp"), P(seq, "tp"), P(seq + ("tp",), None), P(), P(seq), P(seq))
    out_specs = P(seq, "tp")
    return jax.shard_map(
        per_device, mesh=fine, in_specs=in_specs, out_specs=out_specs, check_vma=False
    )
```

profile of v0, /device:TPU:1, one launch (start us, length us, event | category | flops | bytes accessed | tf_op | source)
XLA Modules:
  0.0 202.8 jit_solution(8286302683828630251)
XLA Ops:
  6.5 0.0 copy-start
  6.5 0.0 copy-start.2
  6.5 0.0 all-gather.3.cloned.1.call-start
  6.5 12.4 %all_to_all.19 = bf16[4,4,1024]{2,0,1:T(4,128)(2,1)S(1)} all-to-all(bf16[4,4,1024]{2,0,1:T(4,128)(2,1)} %bitcast.71), channel_id=1, replica_groups=mesh['x'=4,'zh'=2,'y'=8,'core'=2,'tp'=4] {'tp'}, dimensions={1} | all-to-all | bytes 65536 | tf_op jit(solution)/shard_map/all_to_all | solution.py:67
  19.0 0.6 all_to_all.17
  19.6 0.0 all-gather.3.cloned.1.call-update
  19.6 0.0 all-gather.5.cloned.1.call-start
  19.7 137.8 %all-gather.3.cloned.1.call-done = bf16[1024,1024]{1,0:T(8,128)(2,1)} async-done(((bf16[16,1024]{1,0:T(8,128)(2,1)}), bf16[1024,1024]{1,0:T(8,128)(2,1)}) %all-gather.3.cloned.1.call-update) | async-done | bytes 2097168 | tf_op jit(solution)/shard_map/all_gather | solution.py:73
  157.5 0.0 all-gather.5.cloned.1.call-update
  157.5 0.8 reduce-window.4
  158.3 0.6 slice.16
  158.9 1.1 reshape.140
  160.0 1.1 copy.31
  161.2 0.7 broadcast_clamp_fusion
  161.9 0.0 copy-done
  161.9 13.2 %gather_fusion = s32[2048]{0:T(1024)S(1)} fusion(s32[512]{0:T(512)S(1)} %copy-done, s32[2048]{0:T(1024)S(1)} %broadcast_clamp_fusion), kind=kCustom, calls=%fused_computation | custom fusion | bytes 24576 | tf_op jit(solution)/shard_map/jit(_take)/gather | solution.py:76
  175.1 0.7 iota_compare_fusion.3
  175.7 0.1 convert_reduce_fusion
  175.8 0.0 copy-done.2
  175.8 0.1 select_reduce_fusion
  175.9 0.1 fusion.22
  176.0 0.3 fusion.27
  176.3 0.3 compare_and_fusion
  176.6 4.1 %all-gather.5.cloned.1.call-done = bf16[2048,1024]{1,0:T(8,128)(2,1)} async-done(((bf16[1024,1024]{1,0:T(8,128)(2,1)}), bf16[2048,1024]{1,0:T(8,128)(2,1)}) %all-gather.5.cloned.1.call-update) | async-done | bytes 4194320 | tf_op jit(solution)/shard_map/all_gather | solution.py:73
  180.7 6.5 %copy.28 = bf16[2048,1024]{0,1:T(8,128)(2,1)} copy(bf16[2048,1024]{1,0:T(8,128)(2,1)} %all-gather.5.cloned.1.call-done) | data formatting | bytes 8388608 | tf_op jit(solution)/shard_map/all_gather | solution.py:73
  187.3 0.0 copy-start.1
  187.3 3.3 %fusion = (f32[128,4,2]{0,2,1:T(2,128)S(1)}, f32[4,2048,128,2]{2,1,3,0:T(8,128)S(1)}) fusion(pred[128,2048]{0,1:T(8,128)(4,1)S(1)} %compare_and_fusion, bf16[128,4,2,128]{3,2,1,0:T(2,128)(2,1)S(1)} %reshape.140, bf16[2048,4,2,128]{0,3,2,1:T(8,128)(2,1)} %bitcast.65), kind=kOutput, calls=%fused_computation.3 | convolution fusion | flops 543161344 | bytes 11014144 | tf_op jit(solution)/shard_map/thed,phd->thep/dot_general | solution.py:81
  190.6 0.0 copy-done.1
  190.6 2.1 %fusion.3 = f32[4,128,2,128]{1,3,2,0:T(8,128)S(1)} fusion(f32[4,2048,128,2]{2,1,3,0:T(8,128)S(1)} %get-tuple-element.6, f32[128,4,2]{0,2,1:T(2,128)S(1)} %max.7, pred[128,2048]{0,1:T(8,128)(4,1)S(1)} %compare_and_fusion, bf16[2048,4,2,128]{0,3,2,1:T(8,128)(2,1)S(1)} %bitcast.66), kind=kOutput, calls=%fused_computation.6 | convolution fusion | flops 547356672 | bytes 11276288 | tf_op jit(solution)/shard_map/thep,phd->thed/dot_general | solution.py:106
  192.7 2.0 %fusion.1 = f32[128,4,2]{0,2,1:T(2,128)S(1)} fusion(f32[4,2048,128,2]{2,1,3,0:T(8,128)S(1)} %get-tuple-element.6, f32[128,4,2]{0,2,1:T(2,128)S(1)} %max.7, pred[128,2048]{0,1:T(8,128)(4,1)S(1)} %compare_and_fusion), kind=kLoop, calls=%fused_computation.4 | loop fusion | flops 10484736 | bytes 8658944 | tf_op jit(solution)/shard_map/reduce_sum | solution.py:105
  194.7 0.1 fusion.13
  194.9 0.3 fusion.12
  195.1 0.9 copy.38
  (2 shorter events, 0.0 us)
Async XLA Ops:
  6.5 155.3 %copy-start = (s32[512]{0:T(512)S(1)}, s32[512]{0:T(512)}, u32[]{:S(2)}) copy-start(s32[512]{0:T(512)} %param.10) | copy-start | bytes 6148
  6.5 169.3 %copy-start.2 = (s32[4]{0:T(128)S(1)}, s32[4]{0:T(128)}, u32[]{:S(2)}) copy-start(s32[4]{0:T(128)} %param.12) | copy-start | bytes 52
  6.5 150.9 %all-gather.3.cloned.1.call-start = ((), (), s32[]{:S(2)}) async-start(), calls=%async_computation.1 | async-start | bytes 2129920 | tf_op jit(solution)/shard_map/all_gather | solution.py:73
  19.6 161.1 %all-gather.5.cloned.1.call-start = ((), (), s32[]{:S(2)}) async-start(), calls=%async_computation.2 | async-start | bytes 6291456 | tf_op jit(solution)/shard_map/all_gather | solution.py:73
  187.3 3.4 %copy-start.1 = (bf16[2048,1024]{0,1:T(8,128)(2,1)S(1)}, bf16[2048,1024]{0,1:T(8,128)(2,1)}, u32[]{:S(2)}) copy-start(bf16[2048,1024]{0,1:T(8,128)(2,1)} %copy.28) | copy-start | bytes 12582916
Sparse Core Ops, SparseCore 0:
  19.7 137.6 all-gather.2
  159.6 21.1 all-gather.4
where the time goes:
time: 203 us
  waiting for transfers between devices  142 us (70%)
  local copies, waits for them, and re-layouts  24 us (12%)
  between operations  13.5 us (7%)
  blocking collectives  12.4 us (6%)
  matrix products  5.95 us (3%)
  other arithmetic  4.94 us (2%)
    all_gather x2, waiting for transfers between devices, per_device(): mine = lax.all_gather(mine, stage, axis=0, tiled=True)  142 us
    gather x1, local copies, waits for them, and re-layouts, per_device(): owners = jnp.take(block_prefix, table)  13.2 us
    all_to_all x1, blocking collectives, per_device(): lax.all_to_all(prefix_cache, 'tp', split_axis=1, concat_axis=0, tiled=True)  12.4 us
    all_gather x1, local copies, waits for them, and re-layouts, per_device(): mine = lax.all_gather(mine, stage, axis=0, tiled=True)  6.52 us
  transfers between devices with their start and end apart: 2, of which 2 were waited for; matrix products, arithmetic and copies ran while one was open for 9% of the time, Pallas kernels for 0%

commit v1 on v0

--- a/solution.py
+++ b/solution.py
@@ -70,7 +70,8 @@
         start = lax.axis_index("tp") * column_count
         mine = lax.dynamic_slice_in_dim(whole, start, column_count, 1)
     for stage in STAGES:
-        mine = lax.all_gather(mine, stage, axis=0, tiled=True)
+        sent = jnp.stack([mine] * lax.axis_size(stage))
+        mine = jnp.concatenate(lax.all_to_all(sent, stage, 0, 0), axis=0)
     cached = mine.reshape(-1, local_heads, 2, HEAD)
     table = jnp.asarray(block_table(STAGES, block_rows, tensor_count))
     owners = jnp.take(block_prefix, table)

time: 203 us -> 130 us (0.64)
  waiting for transfers between devices: 142 us -> 31.5 us
  local copies, waits for them, and re-layouts: 24 us -> 45 us
  starting transfers between devices: 0.04 us -> 16 us
  between operations: 13.5 us -> 0.12 us
  blocking collectives: 12.4 us -> 24.9 us
    all_gather x2 -> x0, waiting for transfers between devices: 142 us -> none  [per_device(): mine = lax.all_gather(mine, stage, axis=0, tiled=True)]
    all_to_all x0 -> x1, waiting for transfers between devices: none -> 31.5 us  [per_device(): mine = jnp.concatenate(lax.all_to_all(sent, stage, 0, 0), axis=0)]
    all_to_all x0 -> x1, starting transfers between devices: none -> 16 us  [per_device(): mine = jnp.concatenate(lax.all_to_all(sent, stage, 0, 0), axis=0)]
    all_to_all x0 -> x1, blocking collectives: none -> 12.4 us  [per_device(): mine = jnp.concatenate(lax.all_to_all(sent, stage, 0, 0), axis=0)]
    slice x0 -> x1, local copies, waits for them, and re-layouts: none -> 9.77 us  [per_device(): cached[:, :, 1]]
    another operation x0 -> x3, local copies, waits for them, and re-layouts: none -> 9.34 us  [the longest x1 7.71 us: per_device(): cached = mine.reshape(-1, local_heads, 2, HEAD)]
    unnamed x7 -> x6, local copies, waits for them, and re-layouts: 1.13 us -> 10.1 us
    all_gather x1 -> x0, local copies, waits for them, and re-layouts: 6.52 us -> none  [per_device(): mine = lax.all_gather(mine, stage, axis=0, tiled=True)]
  transfers between devices with their start and end apart: 2 -> 1, of which waited for: 2 -> 1; matrix products, arithmetic and copies ran while one was open for 9% -> 15% of each run, Pallas kernels for 0% -> 0%
where the time goes in v1:
time: 130 us; the launch traced here: 129 us
  local copies, waits for them, and re-layouts  45 us (35%)
  waiting for transfers between devices  31.5 us (24%)
  blocking collectives  24.9 us (19%)
  starting transfers between devices  16 us (12%)
  matrix products  6.37 us (5%)
  other arithmetic  5.3 us (4%)
    all_to_all x1, waiting for transfers between devices, per_device(): mine = jnp.concatenate(lax.all_to_all(sent, stage, 0, 0), axis=0)  31.5 us
    all_to_all x1, starting transfers between devices, per_device(): mine = jnp.concatenate(lax.all_to_all(sent, stage, 0, 0), axis=0)  16 us
    gather x1, local copies, waits for them, and re-layouts, per_device(): owners = jnp.take(block_prefix, table)  13.2 us
    all_to_all x1, blocking collectives, per_device(): mine = jnp.concatenate(lax.all_to_all(sent, stage, 0, 0), axis=0)  12.4 us
    all_to_all x1, blocking collectives, per_device(): lax.all_to_all(prefix_cache, 'tp', split_axis=1, concat_axis=0, tiled=True)  12.4 us
    unnamed x6, local copies, waits for them, and re-layouts  10.1 us
    slice x1, local copies, waits for them, and re-layouts, per_device(): cached[:, :, 1]  9.77 us
    another operation x1, local copies, waits for them, and re-layouts, per_device(): cached = mine.reshape(-1, local_heads, 2, HEAD)  7.71 us
  transfers between devices with their start and end apart: 1, of which 1 were waited for; matrix products, arithmetic and copies ran while one was open for 15% of the time, Pallas kernels for 0%

profile of v1, /device:TPU:1, one launch (start us, length us, event | category | flops | bytes accessed | tf_op | source)
XLA Modules:
  0.0 129.1 jit_solution(12570581258516083177)
XLA Ops:
  0.0 0.0 copy-start
  0.0 0.0 copy-start.1
  0.0 12.4 %all_to_all.26 = bf16[4,4,1024]{2,0,1:T(4,128)(2,1)S(1)} all-to-all(bf16[4,4,1024]{2,0,1:T(4,128)(2,1)} %bitcast.75), channel_id=1, replica_groups=mesh['x'=4,'zh'=2,'y'=8,'core'=2,'tp'=4] {'tp'}, dimensions={1} | all-to-all | bytes 65536 | tf_op jit(solution)/shard_map/all_to_all | solution.py:67
  12.5 1.6 %stack.7 = bf16[64,16,1024]{2,1,0:T(8,128)(2,1)} broadcast(bf16[16,1024]{1,0:T(8,128)(2,1)S(1)} %stack.6), dimensions={1,2} | broadcast | bytes 2129920 | tf_op jit(solution)/shard_map/stack | solution.py:73
  14.1 16.0 %all-to-all-start.1 = ((bf16[64,16,1024]{2,1,0:T(8,128)(2,1)}), bf16[64,16,1024]{2,1,0:T(8,128)(2,1)S(1)}, u32[]{:S(2)}, u32[]{:S(2)}) async-start(bf16[64,16,1024]{2,1,0:T(8,128)(2,1)} %stack.7), calls=%async_computation.1 | async-start | bytes 4194304 | tf_op jit(solution)/shard_map/all_to_all | solution.py:74
  30.1 0.8 reduce-window.4
  30.9 0.6 slice.16
  31.5 1.1 reshape.139
  32.6 1.1 copy.30
  33.8 0.7 broadcast_clamp_fusion
  34.5 0.0 copy-done
  34.5 13.2 %gather_fusion = s32[2048]{0:T(1024)S(1)} fusion(s32[512]{0:T(512)S(1)} %copy-done, s32[2048]{0:T(1024)S(1)} %broadcast_clamp_fusion), kind=kCustom, calls=%fused_computation | custom fusion | bytes 24576 | tf_op jit(solution)/shard_map/jit(_take)/gather | solution.py:77
  47.7 0.7 iota_compare_fusion.3
  48.3 0.1 convert_reduce_fusion
  48.4 0.0 copy-done.1
  48.4 0.1 select_reduce_fusion
  48.5 0.1 fusion.28
  48.6 0.3 fusion.34
  48.9 0.3 compare_and_fusion
  49.2 31.5 %all-to-all-done.1 = bf16[64,16,1024]{2,1,0:T(8,128)(2,1)S(1)} async-done(((bf16[64,16,1024]{2,1,0:T(8,128)(2,1)}), bf16[64,16,1024]{2,1,0:T(8,128)(2,1)S(1)}, u32[]{:S(2)}, u32[]{:S(2)}) %all-to-all-start.1) | async-done | bytes 2097184 | tf_op jit(solution)/shard_map/all_to_all | solution.py:74
  80.7 0.4 pad_maximum_fusion
  81.1 12.4 %all_to_all.27 = bf16[2,1024,1024]{2,1,0:T(8,128)(2,1)} all-to-all(bf16[2,1024,1024]{2,1,0:T(8,128)(2,1)S(1)} %pad_maximum_fusion), channel_id=1, replica_groups=mesh['x'=4,'zh'=2,'y'=8,'core'=2,'tp'=4] {'core'}, dimensions={0} | all-to-all | bytes 8388608 | tf_op jit(solution)/shard_map/all_to_all | solution.py:74
  93.5 7.7 %reshape_reshape.3 = bf16[2048,4,2,128]{3,2,1,0:T(2,128)(2,1)} reshape(bf16[2,1024,1024]{2,1,0:T(8,128)(2,1)} %all_to_all.27) | data formatting | bytes 8388608 | tf_op jit(solution)/shard_map/reshape;reshape | solution.py:75
  101.2 9.8 %fusion.33 = (bf16[2048,4,1,128]{3,2,1,0:T(2,128)(2,1)}, bf16[2048,4,1,128]{3,2,1,0:T(2,128)(2,1)}) fusion(bf16[2048,4,2,128]{3,2,1,0:T(2,128)(2,1)} %reshape_reshape.3), kind=kLoop, calls=%fused_computation.46 | loop fusion | bytes 8388608 | tf_op jit(solution)/shard_map/slice | solution.py:110
  111.0 9.0 %copy.43 = bf16[2048,4,1,128]{0,3,1,2:T(8,128)(2,1)S(1)} copy(bf16[2048,4,1,128]{3,2,1,0:T(2,128)(2,1)} %get-tuple-element.5) | data formatting | bytes 4194304
  120.0 3.7 %fusion = (f32[128,4,2]{0,2,1:T(2,128)S(1)}, f32[4,2048,128,2]{2,1,3,0:T(8,128)S(1)}) fusion(pred[128,2048]{0,1:T(8,128)(4,1)S(1)} %compare_and_fusion, bf16[128,4,2,128]{3,2,1,0:T(2,128)(2,1)S(1)} %reshape.139, bf16[2048,4,1,128]{3,2,1,0:T(2,128)(2,1)} %get-tuple-element.6), kind=kOutput, calls=%fused_computation.3 | convolution fusion | flops 543161344 | bytes 11014144 | tf_op jit(solution)/shard_map/thed,phd->thep/dot_general | solution.py:82
  123.7 2.0 %fusion.1 = f32[128,4,2]{0,2,1:T(2,128)S(1)} fusion(f32[4,2048,128,2]{2,1,3,0:T(8,128)S(1)} %get-tuple-element.8, f32[128,4,2]{0,2,1:T(2,128)S(1)} %max.7, pred[128,2048]{0,1:T(8,128)(4,1)S(1)} %compare_and_fusion), kind=kLoop, calls=%fused_computation.4 | loop fusion | flops 10484736 | bytes 8658944 | tf_op jit(solution)/shard_map/reduce_sum | solution.py:106
  125.7 2.1 %fusion.13 = f32[128,4,2,128]{0,3,2,1:T(8,128)S(1)} fusion(f32[4,2048,128,2]{2,1,3,0:T(8,128)S(1)} %get-tuple-element.8, f32[128,4,2]{0,2,1:T(2,128)S(1)} %max.7, pred[128,2048]{0,1:T(8,128)(4,1)S(1)} %compare_and_fusion, bf16[2048,4,1,128]{0,3,1,2:T(8,128)(2,1)S(1)} %copy.43), kind=kOutput, calls=%fused_computation.19 | convolution fusion | flops 547356672 | bytes 11276288 | tf_op jit(solution)/shard_map/thep,phd->thed/dot_general | solution.py:107
  127.9 0.1 fusion.19
  128.0 0.3 fusion.18
  128.3 0.9 copy.36
  (3 shorter events, 0.0 us)
Async XLA Ops:
  0.0 34.5 %copy-start = (s32[512]{0:T(512)S(1)}, s32[512]{0:T(512)}, u32[]{:S(2)}) copy-start(s32[512]{0:T(512)} %param.10) | copy-start | bytes 6148
  0.0 48.4 %copy-start.1 = (s32[4]{0:T(128)S(1)}, s32[4]{0:T(128)}, u32[]{:S(2)}) copy-start(s32[4]{0:T(128)} %param.12) | copy-start | bytes 52
  14.1 66.7 %all-to-all-start.1 = ((bf16[64,16,1024]{2,1,0:T(8,128)(2,1)}), bf16[64,16,1024]{2,1,0:T(8,128)(2,1)S(1)}, u32[]{:S(2)}, u32[]{:S(2)}) async-start(bf16[64,16,1024]{2,1,0:T(8,128)(2,1)} %stack.7), calls=%async_computation.1 | async-start | bytes 4194304 | tf_op jit(solution)/shard_map/all_to_all | solution.py:74

commit v2 on v0

--- a/solution.py
+++ b/solution.py
@@ -12,6 +12,12 @@
 SEQ_PARTS = (("x", 4), ("zh", 2), ("y", 8), ("core", 2))
 STAGES = (("x", "zh", "y"), ("core",))
 TP_FIRST = "a2a"
+
+
+def clusters_balance(m):
+    return jnp.concatenate(
+        lax.all_to_all(jnp.stack(jnp.split(m, lax.axis_size("tp"), 1)), "tp", 0, 0), 0
+    )
 
 
 def block_table(stages, per_block_rows, tensor_count):
@@ -64,7 +70,7 @@
         request_lengths, request_prefix, token_rows
     )
     if TP_FIRST == "a2a":
-        mine = lax.all_to_all(prefix_cache, "tp", split_axis=1, concat_axis=0, tiled=True)
+        mine = clusters_balance(prefix_cache)
     else:
         whole = lax.all_gather(prefix_cache, "tp", axis=0, tiled=True)
         start = lax.axis_index("tp") * column_count

time: 203 us -> 204 us (level)
  no operation moved by 1% of the time
where the time goes in v2:
time: 204 us; the launch traced here: 203 us
  waiting for transfers between devices  142 us (70%)
  local copies, waits for them, and re-layouts  24.8 us (12%)
  between operations  13.5 us (7%)
  blocking collectives  12.1 us (6%)
  matrix products  5.95 us (3%)
  other arithmetic  4.98 us (2%)
    all_gather x2, waiting for transfers between devices, per_device(): mine = lax.all_gather(mine, stage, axis=0, tiled=True)  142 us
    gather x1, local copies, waits for them, and re-layouts, per_device(): owners = jnp.take(block_prefix, table)  13.2 us
    all_to_all x1, blocking collectives, clusters_balance(): lax.all_to_all(jnp.stack(jnp.split(m, lax.axis_size('tp'), 1)), 'tp', 0, 0)  12.1 us
    all_gather x1, local copies, waits for them, and re-layouts, per_device(): mine = lax.all_gather(mine, stage, axis=0, tiled=True)  6.52 us
  transfers between devices with their start and end apart: 2, of which 2 were waited for; matrix products, arithmetic and copies ran while one was open for 9% of the time, Pallas kernels for 0%

profile of v2, /device:TPU:1, one launch (start us, length us, event | category | flops | bytes accessed | tf_op | source)
XLA Modules:
  0.0 203.3 jit_solution(12531746443858411171)
XLA Ops:
  6.5 0.0 copy-start
  6.5 0.0 copy-start.2
  6.5 0.0 all-gather.3.cloned.1.call-start
  6.5 0.8 slice_bitcast_fusion.13
  7.4 12.1 %all_to_all.5 = bf16[4,4,1024]{2,1,0:T(4,128)(2,1)S(1)} all-to-all(bf16[4,4,1024]{2,1,0:T(4,128)(2,1)S(1)} %pad_maximum_fusion), channel_id=1, replica_groups=mesh['x'=4,'zh'=2,'y'=8,'core'=2,'tp'=4] {'tp'}, dimensions={0} | all-to-all | bytes 65536 | tf_op jit(solution)/shard_map/all_to_all | solution.py:19
  19.5 0.6 reshape.139
  20.1 0.0 all-gather.3.cloned.1.call-update
  20.1 0.0 all-gather.5.cloned.1.call-start
  20.2 137.8 %all-gather.3.cloned.1.call-done = bf16[1024,1024]{1,0:T(8,128)(2,1)} async-done(((bf16[16,1024]{1,0:T(8,128)(2,1)}), bf16[1024,1024]{1,0:T(8,128)(2,1)}) %all-gather.3.cloned.1.call-update) | async-done | bytes 2097168 | tf_op jit(solution)/shard_map/all_gather | solution.py:79
  158.0 0.0 all-gather.5.cloned.1.call-update
  158.0 0.8 reduce-window.4
  158.8 0.6 slice.16
  159.4 1.1 reshape.141
  160.5 1.1 copy.41
  161.6 0.7 broadcast_clamp_fusion
  162.4 0.0 copy-done
  162.4 13.2 %gather_fusion = s32[2048]{0:T(1024)S(1)} fusion(s32[512]{0:T(512)S(1)} %copy-done, s32[2048]{0:T(1024)S(1)} %broadcast_clamp_fusion), kind=kCustom, calls=%fused_computation | custom fusion | bytes 24576 | tf_op jit(solution)/shard_map/jit(_take)/gather | solution.py:82
  175.5 0.7 iota_compare_fusion.3
  176.2 0.1 convert_reduce_fusion
  176.3 0.0 copy-done.2
  176.3 0.1 select_reduce_fusion
  176.4 0.1 fusion.25
  176.5 0.3 fusion.30
  176.8 0.3 compare_and_fusion
  177.1 4.1 %all-gather.5.cloned.1.call-done = bf16[2048,1024]{1,0:T(8,128)(2,1)} async-done(((bf16[1024,1024]{1,0:T(8,128)(2,1)}), bf16[2048,1024]{1,0:T(8,128)(2,1)}) %all-gather.5.cloned.1.call-update) | async-done | bytes 4194320 | tf_op jit(solution)/shard_map/all_gather | solution.py:79
  181.2 6.5 %copy.37 = bf16[2048,1024]{0,1:T(8,128)(2,1)} copy(bf16[2048,1024]{1,0:T(8,128)(2,1)} %all-gather.5.cloned.1.call-done) | data formatting | bytes 8388608 | tf_op jit(solution)/shard_map/all_gather | solution.py:79
  187.8 0.0 copy-start.1
  187.8 3.3 %fusion = (f32[128,4,2]{0,2,1:T(2,128)S(1)}, f32[4,2048,128,2]{2,1,3,0:T(8,128)S(1)}) fusion(pred[128,2048]{0,1:T(8,128)(4,1)S(1)} %compare_and_fusion, bf16[128,4,2,128]{3,2,1,0:T(2,128)(2,1)S(1)} %reshape.141, bf16[2048,4,2,128]{0,3,2,1:T(8,128)(2,1)} %bitcast.79), kind=kOutput, calls=%fused_computation.3 | convolution fusion | flops 543161344 | bytes 11014144 | tf_op jit(solution)/shard_map/thed,phd->thep/dot_general | solution.py:87
  191.1 0.0 copy-done.1
  191.1 2.1 %fusion.12 = f32[128,4,2,128]{0,3,2,1:T(8,128)S(1)} fusion(f32[4,2048,128,2]{2,1,3,0:T(8,128)S(1)} %get-tuple-element.10, f32[128,4,2]{0,2,1:T(2,128)S(1)} %max.7, pred[128,2048]{0,1:T(8,128)(4,1)S(1)} %compare_and_fusion, bf16[2048,4,2,128]{0,3,2,1:T(8,128)(2,1)S(1)} %bitcast.80), kind=kOutput, calls=%fused_computation.18 | convolution fusion | flops 547356672 | bytes 11276288 | tf_op jit(solution)/shard_map/thep,phd->thed/dot_general | solution.py:112
  193.2 2.0 %fusion.1 = f32[128,4,2]{0,2,1:T(2,128)S(1)} fusion(f32[4,2048,128,2]{2,1,3,0:T(8,128)S(1)} %get-tuple-element.10, f32[128,4,2]{0,2,1:T(2,128)S(1)} %max.7, pred[128,2048]{0,1:T(8,128)(4,1)S(1)} %compare_and_fusion), kind=kLoop, calls=%fused_computation.4 | loop fusion | flops 10484736 | bytes 8658944 | tf_op jit(solution)/shard_map/reduce_sum | solution.py:111
  195.2 0.1 fusion.16
  195.4 0.3 fusion.15
  195.6 0.9 copy.47
  (3 shorter events, 0.0 us)
Async XLA Ops:
  6.5 155.8 %copy-start = (s32[512]{0:T(512)S(1)}, s32[512]{0:T(512)}, u32[]{:S(2)}) copy-start(s32[512]{0:T(512)} %param.10) | copy-start | bytes 6148
  6.5 169.8 %copy-start.2 = (s32[4]{0:T(128)S(1)}, s32[4]{0:T(128)}, u32[]{:S(2)}) copy-start(s32[4]{0:T(128)} %param.12) | copy-start | bytes 52
  6.5 151.4 %all-gather.3.cloned.1.call-start = ((), (), s32[]{:S(2)}) async-start(), calls=%async_computation.1 | async-start | bytes 2129920 | tf_op jit(solution)/shard_map/all_gather | solution.py:79
  20.1 161.1 %all-gather.5.cloned.1.call-start = ((), (), s32[]{:S(2)}) async-start(), calls=%async_computation.2 | async-start | bytes 6291456 | tf_op jit(solution)/shard_map/all_gather | solution.py:79
  187.8 3.4 %copy-start.1 = (bf16[2048,1024]{0,1:T(8,128)(2,1)S(1)}, bf16[2048,1024]{0,1:T(8,128)(2,1)}, u32[]{:S(2)}) copy-start(bf16[2048,1024]{0,1:T(8,128)(2,1)} %copy.37) | copy-start | bytes 12582916
Sparse Core Ops, SparseCore 0:
  20.2 137.6 all-gather.2
  160.1 21.1 all-gather.4
